TPU v7x, 32 devices: a whole 2x2x4 slice. The times are simulated.
32 devices in a mesh: tm: 4 (over y, x), height: 2 (over core), chan: 4 (over z).
Axes of the slice: x: 2, y: 2, z: 4, core: 2. Of those that a mesh axis runs over, the one named last changes fastest.
Arguments:
- features: bfloat16 [384, 8, 8, 160], P('chan', 'tm', 'height'), may hold values from -400 to 400, as said below
- cotangent: bfloat16 [384, 8, 8, 160], P('chan', 'tm', 'height'), may hold values from -6 to 6
- conv_weight: bfloat16 [384, 27, 384], P('chan'), may hold values from -0.0625 to 0.0625
- norm_gain: float32 [384], replicated, may hold values from 0.5 to 1.5
- norm_bias: float32 [384], replicated, may hold values from -3 to 3
Outputs:
- input_grad: bfloat16 [384, 8, 8, 160], P('chan', 'tm', 'height')
- weight_grad: float32 [384, 27, 384], P('chan')
Inputs may be any that keep to these rules, and one draw needn't show every extreme that they name: `features`: bounded activations.
All inputs are finite; a program needn't handle non-finite values.
Results may differ from a plain program's by a relative error of at most 0.003.
Values may be sent and summed in bfloat16 or wider, within the bound.
No kernel may reach another device: no remote copies, remote signals or barrier semaphores. Data moves between devices by JAX's collectives and lax.ppermute only.
A program may use at most 64 MiB of HBM per device.

v0:
```python
import math
import jax
import jax.numpy as jnp
from jax import lax
from jax.sharding import PartitionSpec as P


def from_behind(block, axis, distance):
    devices = range(lax.axis_size(axis))
    route = [(i - distance, i) for i in devices if i - distance in devices]
    return lax.ppermute(block, axis, route)


def with_halo(array, sides, width):
    for axis, dim in sides:
        size, length = (lax.axis_size(axis), array.shape[dim])
        up = [(i, (i + 1) % size) for i in range(size - 1)]
        down = [(j, i) for i, j in up]
        last = lax.slice_in_dim(array, length - width, length, axis=dim)
        first = lax.slice_in_dim(array, 0, width, axis=dim)
        before = lax.ppermute(last, axis, up)
        after = lax.ppermute(first, axis, down)
        array = jnp.concatenate([before, array, after], axis=dim)
    return array


def on_device(features, cotangent, conv_weight, norm_gain, norm_bias):
    chans, frames, rows, cols = features.shape
    whole_x = lax.all_gather(features, "chan", axis=0, tiled=True)
    total = whole_x.shape[0]
    flat_x = whole_x.reshape(total, -1).astype(jnp.float32)
    inv_rms = lax.rsqrt(jnp.mean(flat_x * flat_x, axis=0, keepdims=True) + 1e-06)
    normed = flat_x * inv_rms * norm_gain[:, None] + norm_bias[:, None]
    active = jax.nn.silu(normed).astype(jnp.bfloat16)
    ahead = from_behind(cotangent, "tm", -1)
    longer = jnp.concatenate([cotangent, ahead], axis=1)
    bordered = with_halo(longer, (("height", 2),), 1)
    padded = jnp.pad(bordered, ((0, 0), (0, 0), (0, 0), (1, 1)))
    taps = []
    for kt in range(3):
        for kh in range(3):
            for kw in range(3):
                taps.append(
                    padded[
                        :, 2 - kt : 2 - kt + frames, 2 - kh : 2 - kh + rows, 2 - kw : 2 - kw + cols
                    ]
                )
    stacked = jnp.stack(taps, axis=1).reshape(chans * 27, -1)
    local_sums = lax.dot_general(
        stacked, active, (((1,), (1,)), ((), ())), preferred_element_type=jnp.float32
    )
    positions = frames * lax.axis_size("tm") * rows * lax.axis_size("height") * cols
    summed = lax.psum(local_sums, ("tm", "height"))
    weight_grad = (summed / math.sqrt(positions)).reshape(chans, 27, total)
    sig = jax.nn.sigmoid(normed)
    slope = sig * (1.0 + normed * (1.0 - sig))
    offset = lax.axis_index("chan") * chans
    weight_part = conv_weight.reshape(chans * 27, chans * lax.axis_size("chan"))
    act_grad = lax.psum_scatter(
        lax.dot_general(
            weight_part, stacked, (((0,), (0,)), ((), ())), preferred_element_type=jnp.float32
        ),
        "chan",
        scatter_dimension=0,
        tiled=True,
    )
    own_x = features.reshape(chans, -1).astype(jnp.float32)
    own_slope = lax.dynamic_slice_in_dim(slope, offset, chans, 0)
    own_gain = lax.dynamic_slice_in_dim(norm_gain, offset, chans, 0)
    upstream = act_grad * own_slope * own_gain[:, None]
    dots = lax.psum(jnp.sum(upstream * own_x, axis=0, keepdims=True), "chan")
    own_back = inv_rms * upstream - own_x * inv_rms**3 * dots / total
    result = cotangent.reshape(chans, -1).astype(jnp.float32) + own_back
    return (result.astype(jnp.bfloat16).reshape(features.shape), weight_grad)


def solution(mesh):
    return jax.shard_map(
        on_device,
        mesh=mesh,
        in_specs=(
            P("chan", "tm", "height", None),
            P("chan", "tm", "height", None),
            P("chan", None, None),
            P(),
            P(),
        ),
        out_specs=(P("chan", "tm", "height", None), P("chan", None, None)),
        check_vma=False,
    )
```

profile of v0, /device:TPU:0, one launch (start us, length us, event | category | flops | bytes accessed | tf_op | source)
XLA Modules:
  0.0 245.2 jit_solution(13448478375143645336)
XLA Ops:
  8.0 0.0 all-reduce.3.cloned.1.call-start
  8.0 1.3 collective-permute-start
  9.3 1.3 copy.16
  10.7 31.4 %all_gather.3 = bf16[384,2,4,160]{3,2,1,0:T(4,128)(2,1)S(1)} all-gather(bf16[96,2,4,160]{3,2,1,0:T(4,128)(2,1)S(1)} %copy.16), channel_id=1, replica_groups=mesh['tm'=4,'height'=2,'chan'=4] {'chan'}, dimensions={0}, use_global_device_ids=true | all-gather | bytes 1228800 | tf_op jit(solution)/shard_map/all_gather | solution.py:29
  42.1 1.4 copy.17
  43.5 0.4 multiply_reduce_fusion
  43.9 1.0 constant_dynamic-update-slice_fusion.1
  44.9 0.0 collective-permute-done
  45.0 1.3 collective-permute-start.1
  46.3 1.3 collective-permute-start.2
  47.6 1.4 multiply_convert_fusion
  49.0 0.0 collective-permute-done.1
  49.0 0.6 collective-permute-done.2
  49.6 0.3 fusion.7
  50.0 0.0 copy-start
  50.0 0.8 fusion.53
  50.8 0.8 fusion.30
  51.6 0.7 fusion.52
  52.4 0.8 fusion.51
  53.2 0.7 bitcast_dynamic-update-slice_fusion.1
  53.9 0.8 fusion.50
  54.7 0.8 fusion.49
  55.5 0.8 fusion.24
  56.3 0.8 fusion.48
  57.1 0.8 fusion.47
  57.9 0.8 fusion.27
  58.7 0.7 fusion.46
  59.5 0.8 fusion.45
  60.3 0.8 fusion.44
  61.1 0.8 fusion.43
  61.8 0.8 fusion.42
  62.6 0.8 fusion.21
  63.4 0.8 fusion.41
  64.2 0.8 fusion.40
  65.0 0.8 fusion.39
  65.8 0.8 fusion.37
  66.6 0.8 fusion.36
  67.4 0.0 copy-done
  67.4 0.7 bitcast_dynamic-update-slice_fusion
  68.2 0.8 fusion.35
  68.9 0.8 fusion.34
  69.7 0.8 fusion.33
  70.6 0.8 fusion.31
  71.3 21.1 %copy.18 = bf16[96,27,2,4,160]{4,3,2,1,0:T(4,128)(2,1)} copy(bf16[96,27,2,4,160]{0,4,3,2,1:T(8,128)(2,1)} %fusion.31) | data formatting | bytes 13271040 | tf_op jit(solution)/shard_map/stack | solution.py:48
  92.5 20.4 %reshape.67 = bf16[2592,1280]{1,0:T(8,128)(2,1)} reshape(bf16[96,27,2,4,160]{4,3,2,1,0:T(4,128)(2,1)} %copy.18) | data formatting | bytes 13271040 | tf_op jit(solution)/shard_map/reshape | solution.py:48
  112.8 8.4 %fusion.56 = f32[2592,384]{1,0:T(8,128)} fusion(bf16[2592,1280]{1,0:T(8,128)(2,1)} %reshape.67, bf16[384,1280]{0,1:T(8,128)(2,1)S(1)} %bitcast.128), kind=kOutput, calls=%fused_computation.102 | convolution fusion | flops 2548039680 | bytes 11599872 | tf_op jit(solution)/shard_map/dot_general | solution.py:49
  121.3 0.0 all-reduce.3.cloned.1.call-update
  121.3 0.2 reduce-scatter.4.cloned.1.call-start
  121.5 2.3 copy.19
  123.8 2.2 reshape.68
  126.0 6.7 %convolution_bitcast_fusion = f32[384,1280]{0,1:T(8,128)S(1)} fusion(bf16[2592,1280]{1,0:T(8,128)(2,1)} %reshape.67, bf16[2592,384]{1,0:T(8,128)(2,1)} %reshape.68), kind=kOutput, calls=%fused_computation.2 | convolution fusion | flops 2548039680 | bytes 10592256 | tf_op jit(solution)/shard_map/dot_general | solution.py:60
  132.7 1.8 copy.21
  134.5 0.0 reduce-scatter.4.cloned.1.call-update
  134.5 0.1 rsqrt.16
  134.6 0.1 dynamic_slice.7
  134.7 1.8 negate_exponential_fusion
  136.5 66.4 %all-reduce.3.cloned.1.call-done = f32[2592,384]{1,0:T(8,128)} async-done(((f32[2592,384]{1,0:T(8,128)}), f32[2592,384]{1,0:T(8,128)}) %all-reduce.3.cloned.1.call-update) | async-done | bytes 3981328 | tf_op jit(solution)/shard_map/psum | solution.py:53
  202.9 4.4 %broadcast_multiply_fusion = f32[2592,384]{1,0:T(8,128)} fusion(f32[2592,384]{1,0:T(8,128)} %all-reduce.3.cloned.1.call-done), kind=kLoop, calls=%fused_computation.4 | loop fusion | flops 995328 | bytes 7962624 | tf_op jit(solution)/shard_map/div | solution.py:54
  207.3 5.0 %reshape.70 = f32[96,27,384]{2,1,0:T(8,128)} reshape(f32[2592,384]{1,0:T(8,128)} %broadcast_multiply_fusion) | data formatting | bytes 7962624 | tf_op jit(solution)/shard_map/reshape | solution.py:54
  212.3 6.6 %copy.20 = f32[96,27,384]{2,0,1:T(8,128)} copy(f32[96,27,384]{2,1,0:T(8,128)} %reshape.70) | data formatting | bytes 7962624
  218.8 2.1 copy.22
  221.0 2.8 %fusion.13 = (f32[1280]{0:T(1024)S(1)}, f32[96,1280]{0,1:T(8,128)}) fusion(bf16[96,2,4,160]{0,3,2,1:T(8,128)(2,1)S(1)} %copy-done.2, f32[96]{0:T(128)S(1)} %dynamic_slice.7, f32[96,1280]{0,1:T(8,128)} %copy.22, f32[384,1280]{0,1:T(8,128)} %get-tuple-element.13, s32[]{:T(128)S(6)} %select_n.4, f32[384,1280]{0,1:T(8,128)S(1)} %get-tuple-element.12), kind=kLoop, calls=%fused_computation.31 | loop fusion | flops 1350400 | bytes 2217348 | tf_op jit(solution)/shard_map/reduce_sum | solution.py:71
  223.8 11.6 %psum.14 = f32[1280]{0:T(1024)S(1)} all-reduce(f32[1280]{0:T(1024)S(1)} %get-tuple-element.10), channel_id=1, replica_groups=mesh['tm'=4,'height'=2,'chan'=4] {'chan'}, use_global_device_ids=true, to_apply=%region_3.4 | all-reduce | flops 1280 | bytes 10240 | tf_op jit(solution)/shard_map/psum | solution.py:71
  235.4 2.4 fusion.12
  (13 shorter events, 0.1 us)
Async XLA Ops:
  8.0 194.9 %all-reduce.3.cloned.1.call-start = ((), (), s32[]{:S(2)}) async-start(), calls=%async_computation.1 | async-start | bytes 7962624 | tf_op jit(solution)/shard_map/psum | solution.py:53
  8.0 36.9 %collective-permute-start = (bf16[96,2,4,160]{0,3,2,1:T(8,128)(2,1)}, bf16[96,2,4,160]{0,3,2,1:T(8,128)(2,1)S(1)}, u32[]{:S(2)}, u32[]{:S(2)}) collective-permute-start(bf16[96,2,4,160]{0,3,2,1:T(8,128)(2,1)} %param.6), channel_id=1, source_target_pairs={{8,0},{16,8},{24,16},{9,1},{17,9},{25,17},{10,2},{18,10},{26,18},{... | collective-permute-start | bytes 737288 | tf_op jit(solution)/shard_map/ppermute | solution.py:11
  45.0 4.0 %collective-permute-start.1 = (bf16[96,4,1,160]{0,3,2,1:T(8,128)(2,1)S(1)}, bf16[96,4,1,160]{0,3,2,1:T(8,128)(2,1)S(1)}, u32[]{:S(2)}, u32[]{:S(2)}) collective-permute-start(bf16[96,4,1,160]{0,3,2,1:T(8,128)(2,1)S(1)} %get-tuple-element.14), channel_id=1, source_target_pairs={{0,4},{1,5},{2,6},{3,7},{8,12},{9,13},{10,14},{11,15},{16,20},{17,... | collective-permute-start | bytes 368648 | tf_op jit(solution)/shard_map/ppermute | solution.py:21
  46.3 3.3 %collective-permute-start.2 = (bf16[96,4,1,160]{0,3,2,1:T(8,128)(2,1)S(1)}, bf16[96,4,1,160]{0,3,2,1:T(8,128)(2,1)S(1)}, u32[]{:S(2)}, u32[]{:S(2)}) collective-permute-start(bf16[96,4,1,160]{0,3,2,1:T(8,128)(2,1)S(1)} %get-tuple-element.15), channel_id=1, source_target_pairs={{4,0},{5,1},{6,2},{7,3},{12,8},{13,9},{14,10},{15,11},{20,16},{21,... | collective-permute-start | bytes 368648 | tf_op jit(solution)/shard_map/ppermute | solution.py:22
  50.0 17.4 %copy-start = (bf16[96,2,4,160]{0,3,2,1:T(8,128)(2,1)S(1)}, bf16[96,2,4,160]{0,3,2,1:T(8,128)(2,1)}, u32[]{:S(2)}) copy-start(bf16[96,2,4,160]{0,3,2,1:T(8,128)(2,1)} %param.6) | copy-start | bytes 737284
  121.3 97.5 %reduce-scatter.4.cloned.1.call-start = ((), (), s32[]{:S(2)}) async-start(), calls=%async_computation.2 | async-start | bytes 2457600
  126.0 8.6 %copy-start.3 = (f32[384]{0:T(512)S(1)}, f32[384]{0:T(512)}, u32[]{:S(2)}) copy-start(f32[384]{0:T(512)} %param.8) | copy-start | bytes 4612
  126.0 8.7 %copy-start.4 = (f32[384]{0:T(512)S(1)}, f32[384]{0:T(512)}, u32[]{:S(2)}) copy-start(f32[384]{0:T(512)} %param.9) | copy-start | bytes 4612
  207.3 13.7 %copy-start.2 = (bf16[96,2,4,160]{0,3,2,1:T(8,128)(2,1)S(1)}, bf16[96,2,4,160]{0,3,2,1:T(8,128)(2,1)}, u32[]{:S(2)}) copy-start(bf16[96,2,4,160]{0,3,2,1:T(8,128)(2,1)} %param.5) | copy-start | bytes 737284
  207.3 28.1 %copy-start.1 = (bf16[96,2,4,160]{0,3,2,1:T(8,128)(2,1)S(1)}, bf16[96,2,4,160]{0,3,2,1:T(8,128)(2,1)}, u32[]{:S(2)}) copy-start(bf16[96,2,4,160]{0,3,2,1:T(8,128)(2,1)} %param.6) | copy-start | bytes 737284
Sparse Core Ops, SparseCore 0:
  121.4 81.3 all-reduce.2
Sparse Core Ops, SparseCore 1:
  134.6 44.6 reduce-scatter.3
where the time goes:
time: 247 us; the launch traced here: 245 us
  local copies, waits for them, and re-layouts  82 us (33%)
  waiting for transfers between devices  67 us (27%)
  blocking collectives  43 us (17%)
  other arithmetic  18.3 us (7%)
  between operations  15.6 us (6%)
  matrix products  15.1 us (6%)
  starting transfers between devices  4.15 us (2%)
    psum x1, waiting for transfers between devices, on_device(): summed = lax.psum(local_sums, ('tm', 'height'))  66.4 us
    all_gather x1, blocking collectives, on_device(): whole_x = lax.all_gather(features, 'chan', axis=0, tiled=True)  31.4 us
    unnamed x36, local copies, waits for them, and re-layouts  30.9 us
    another operation x2, local copies, waits for them, and re-layouts, on_device(): stacked = jnp.stack(taps, axis=1).reshape(chans * 27, -1)  21.9 us
    reshape x1, local copies, waits for them, and re-layouts, on_device(): stacked = jnp.stack(taps, axis=1).reshape(chans * 27, -1)  20.4 us
    psum x1, blocking collectives, on_device(): dots = lax.psum(jnp.sum(upstream * own_x, axis=0, keepdims=True), 'chan')  11.6 us
    dot_general x1, matrix products, on_device(): lax.dot_general(stacked, active, (((1,), (1,)), ((), ())), preferred_elem...  8.42 us
    dot_general x1, matrix products, on_device(): lax.dot_general(weight_part, stacked, (((0,), (0,)), ((), ())), preferred...  6.67 us
  transfers between devices with their start and end apart: 5, of which 2 were waited for; matrix products, arithmetic and copies ran while one was open for 15% of the time, Pallas kernels for 0%

commit v1 on v0

--- a/solution.py
+++ b/solution.py
@@ -50,7 +50,7 @@
         stacked, active, (((1,), (1,)), ((), ())), preferred_element_type=jnp.float32
     )
     positions = frames * lax.axis_size("tm") * rows * lax.axis_size("height") * cols
-    summed = lax.psum(local_sums, ("tm", "height"))
+    summed = jnp.sum(lax.all_gather(local_sums, ("tm", "height")), axis=0)
     weight_grad = (summed / math.sqrt(positions)).reshape(chans, 27, total)
     sig = jax.nn.sigmoid(normed)
     slope = sig * (1.0 + normed * (1.0 - sig))

time: 247 us -> 368 us (1.49)
  waiting for transfers between devices: 67 us -> 145 us
  blocking collectives: 43 us -> 66.1 us
  other arithmetic: 18.3 us -> 32.5 us
    all_gather x0 -> x1, waiting for transfers between devices: none -> 135 us  [on_device(): summed = jnp.sum(lax.all_gather(local_sums, ('tm', 'height')), axis=0)]
    psum x1 -> x0, waiting for transfers between devices: 66.4 us -> none  [on_device(): summed = lax.psum(local_sums, ('tm', 'height'))]
    all_gather x1, blocking collectives: 31.4 us -> 53.5 us  [on_device(): whole_x = lax.all_gather(features, 'chan', axis=0, tiled=True)]
    reduce_sum x0 -> x1, other arithmetic: none -> 13.9 us  [on_device(): summed = jnp.sum(lax.all_gather(local_sums, ('tm', 'height')), axis=0)]
    ppermute x1, waiting for transfers between devices: 0.01 us -> 10.5 us  [from_behind(): return lax.ppermute(block, axis, route)]
    reshape x1 -> x0, local copies, waits for them, and re-layouts: 4.98 us -> none  [on_device(): weight_grad = (summed / math.sqrt(positions)).reshape(chans, 27, total)]
    div x0 -> x1, local copies, waits for them, and re-layouts: none -> 4.92 us  [on_device(): weight_grad = (summed / math.sqrt(positions)).reshape(chans, 27, total)]
    unnamed x36 -> x42, local copies, waits for them, and re-layouts: 30.9 us -> 32.6 us
  transfers between devices with their start and end apart: 5 -> 5, of which waited for: 2 -> 2; matrix products, arithmetic and copies ran while one was open for 15% -> 7% of each run, Pallas kernels for 0% -> 0%
where the time goes in v1:
time: 368 us; the launch traced here: 366 us
  waiting for transfers between devices  145 us (39%)
  local copies, waits for them, and re-layouts  84.4 us (23%)
  blocking collectives  66.1 us (18%)
  other arithmetic  32.5 us (9%)
  matrix products  16.6 us (5%)
  between operations  15.6 us (4%)
  starting transfers between devices  5.7 us (2%)
    all_gather x1, waiting for transfers between devices, on_device(): summed = jnp.sum(lax.all_gather(local_sums, ('tm', 'height')), axis=0)  135 us
    all_gather x1, blocking collectives, on_device(): whole_x = lax.all_gather(features, 'chan', axis=0, tiled=True)  53.5 us
    unnamed x42, local copies, waits for them, and re-layouts  32.6 us
    another operation x2, local copies, waits for them, and re-layouts, on_device(): stacked = jnp.stack(taps, axis=1).reshape(chans * 27, -1)  21.8 us
    reshape x1, local copies, waits for them, and re-layouts, on_device(): stacked = jnp.stack(taps, axis=1).reshape(chans * 27, -1)  20.5 us
    reduce_sum x1, other arithmetic, on_device(): summed = jnp.sum(lax.all_gather(local_sums, ('tm', 'height')), axis=0)  13.9 us
    psum x1, blocking collectives, on_device(): dots = lax.psum(jnp.sum(upstream * own_x, axis=0, keepdims=True), 'chan')  12.6 us
    ppermute x1, waiting for transfers between devices, from_behind(): return lax.ppermute(block, axis, route)  10.5 us
  transfers between devices with their start and end apart: 5, of which 2 were waited for; matrix products, arithmetic and copies ran while one was open for 7% of the time, Pallas kernels for 0%

profile of v1, /device:TPU:0, one launch (start us, length us, event | category | flops | bytes accessed | tf_op | source)
XLA Modules:
  0.0 366.3 jit_solution(4276430643013541657)
XLA Ops:
  8.0 0.0 reduce-scatter.4.cloned.1.call-start
  8.0 1.3 collective-permute-start
  9.3 1.0 constant_dynamic-update-slice_fusion.1
  10.3 10.5 %collective-permute-done = bf16[96,2,4,160]{0,3,2,1:T(8,128)(2,1)S(1)} collective-permute-done((bf16[96,2,4,160]{0,3,2,1:T(8,128)(2,1)}, bf16[96,2,4,160]{0,3,2,1:T(8,128)(2,1)S(1)}, u32[]{:S(2)}, u32[]{:S(2)}) %collective-permute-start) | collective-permute-done | bytes 245792 | tf_op jit(solution)/shard_map/ppermute | solution.py:11
  20.9 0.8 fusion.55
  21.6 1.3 collective-permute-start.2
  22.9 3.0 collective-permute-start.1
  26.0 2.3 copy.18
  28.3 2.1 reshape.69
  30.4 0.7 copy-done.2
  31.1 0.3 fusion.7
  31.4 0.0 copy-start
  31.4 0.8 fusion.53
  32.3 1.7 fusion.30
  34.0 0.7 fusion.52
  34.7 0.8 fusion.51
  35.5 1.7 bitcast_dynamic-update-slice_fusion.1
  37.2 0.7 fusion.50
  38.0 0.8 fusion.49
  38.8 0.8 fusion.24
  39.6 0.7 fusion.48
  40.4 0.8 fusion.47
  41.2 1.7 fusion.27
  42.8 0.7 fusion.46
  43.6 0.8 fusion.45
  44.4 0.8 fusion.44
  45.2 0.8 fusion.43
  45.9 0.8 fusion.42
  46.8 0.8 fusion.21
  47.5 0.7 fusion.41
  48.3 0.8 fusion.40
  49.1 0.8 fusion.39
  49.9 0.7 fusion.37
  50.6 0.8 fusion.36
  51.4 0.8 bitcast_dynamic-update-slice_fusion
  52.2 0.8 fusion.35
  53.0 0.8 fusion.34
  53.8 0.8 fusion.33
  54.6 0.7 fusion.31
  55.3 21.1 %copy.17 = bf16[96,27,2,4,160]{4,3,2,1,0:T(4,128)(2,1)} copy(bf16[96,27,2,4,160]{0,4,3,2,1:T(8,128)(2,1)} %fusion.31) | data formatting | bytes 13271040 | tf_op jit(solution)/shard_map/stack | solution.py:48
  76.4 20.5 %reshape.68 = bf16[2592,1280]{1,0:T(8,128)(2,1)} reshape(bf16[96,27,2,4,160]{4,3,2,1,0:T(4,128)(2,1)} %copy.17) | data formatting | bytes 13271040 | tf_op jit(solution)/shard_map/reshape | solution.py:48
  97.0 8.1 %convolution_bitcast_fusion = f32[384,1280]{0,1:T(8,128)} fusion(bf16[2592,1280]{1,0:T(8,128)(2,1)} %reshape.68, bf16[2592,384]{1,0:T(8,128)(2,1)S(1)} %copy-done.4), kind=kOutput, calls=%fused_computation.2 | convolution fusion | flops 2548039680 | bytes 10592256 | tf_op jit(solution)/shard_map/dot_general | solution.py:60
  105.0 2.9 copy.20
  108.0 0.0 reduce-scatter.4.cloned.1.call-update
  108.0 0.0 all-gather.3.cloned.1.call-start
  108.1 0.3 copy.15
  108.4 53.5 %all_gather.9 = bf16[384,2,4,160]{3,2,1,0:T(4,128)(2,1)S(1)} all-gather(bf16[96,2,4,160]{3,2,1,0:T(4,128)(2,1)S(1)} %copy.15), channel_id=1, replica_groups=mesh['tm'=4,'height'=2,'chan'=4] {'chan'}, dimensions={0}, use_global_device_ids=true | all-gather | bytes 1228800 | tf_op jit(solution)/shard_map/all_gather | solution.py:29
  161.9 1.4 copy.16
  163.4 0.4 multiply_reduce_fusion
  163.8 0.7 multiply_convert_fusion
  164.5 8.5 %fusion.56 = f32[2592,384]{1,0:T(8,128)} fusion(bf16[2592,1280]{1,0:T(8,128)(2,1)} %reshape.68, bf16[384,1280]{0,1:T(8,128)(2,1)S(1)} %bitcast.130), kind=kOutput, calls=%fused_computation.102 | convolution fusion | flops 2548039680 | bytes 11599872 | tf_op jit(solution)/shard_map/dot_general | solution.py:49
  173.0 0.0 all-gather.3.cloned.1.call-update
  173.0 0.1 rsqrt.16
  173.1 0.1 dynamic_slice.7
  173.1 1.7 negate_exponential_fusion
  174.9 2.1 copy.21
  177.0 2.2 fusion.13
  179.3 12.6 %psum.7 = f32[1280]{0:T(1024)S(1)} all-reduce(f32[1280]{0:T(1024)S(1)} %get-tuple-element.8), channel_id=1, replica_groups=mesh['tm'=4,'height'=2,'chan'=4] {'chan'}, use_global_device_ids=true, to_apply=%region_3.4 | all-reduce | flops 1280 | bytes 10240 | tf_op jit(solution)/shard_map/psum | solution.py:71
  191.8 2.3 fusion.12
  194.1 135.0 %all-gather.3.cloned.1.call-done = f32[20736,384]{1,0:T(8,128)} async-done(((f32[2592,384]{1,0:T(8,128)}), f32[20736,384]{1,0:T(8,128)}) %all-gather.3.cloned.1.call-update) | async-done | bytes 31850512 | tf_op jit(solution)/shard_map/all_gather | solution.py:53
  329.1 13.9 %reduce_sum.29 = f32[2592,384]{1,0:T(8,128)} reduce(f32[8,2592,384]{2,1,0:T(8,128)} %bitcast.129, f32[]{:T(128)} %constant.10.clone.1), dimensions={0}, to_apply=%region_4.5 | reduce | flops 6967296 | bytes 35831812 | tf_op jit(solution)/shard_map/reduce_sum | solution.py:53
  342.9 4.4 %broadcast_multiply_fusion = f32[2592,384]{1,0:T(8,128)} fusion(f32[2592,384]{1,0:T(8,128)} %reduce_sum.29), kind=kLoop, calls=%fused_computation.4 | loop fusion | flops 995328 | bytes 7962624 | tf_op jit(solution)/shard_map/div | solution.py:54
  347.4 4.9 %div.36 = f32[96,27,384]{2,1,0:T(8,128)} reshape(f32[2592,384]{1,0:T(8,128)} %broadcast_multiply_fusion) | data formatting | bytes 7962624 | tf_op jit(solution)/shard_map/div | solution.py:54
  352.3 6.6 %copy.19 = f32[96,27,384]{2,0,1:T(8,128)} copy(f32[96,27,384]{2,1,0:T(8,128)} %div.36) | data formatting | bytes 7962624
  (20 shorter events, 0.1 us)
Async XLA Ops:
  8.0 166.9 %reduce-scatter.4.cloned.1.call-start = ((), (), s32[]{:S(2)}) async-start(), calls=%async_computation.2 | async-start | bytes 2457600
  8.0 12.8 %collective-permute-start = (bf16[96,2,4,160]{0,3,2,1:T(8,128)(2,1)}, bf16[96,2,4,160]{0,3,2,1:T(8,128)(2,1)S(1)}, u32[]{:S(2)}, u32[]{:S(2)}) collective-permute-start(bf16[96,2,4,160]{0,3,2,1:T(8,128)(2,1)} %param.6), channel_id=1, source_target_pairs={{8,0},{16,8},{24,16},{9,1},{17,9},{25,17},{10,2},{18,10},{26,18},{... | collective-permute-start | bytes 737288 | tf_op jit(solution)/shard_map/ppermute | solution.py:11
  20.8 2.1 copy-start.5
  21.6 8.8 %collective-permute-start.2 = (bf16[96,4,1,160]{0,3,2,1:T(8,128)(2,1)}, bf16[96,4,1,160]{0,3,2,1:T(8,128)(2,1)S(1)}, u32[]{:S(2)}, u32[]{:S(2)}) collective-permute-start(bf16[96,4,1,160]{0,3,2,1:T(8,128)(2,1)} %get-tuple-element.13), channel_id=1, source_target_pairs={{4,0},{5,1},{6,2},{7,3},{12,8},{13,9},{14,10},{15,11},{20,16},{21,... | collective-permute-start | bytes 368648 | tf_op jit(solution)/shard_map/ppermute | solution.py:22
  22.9 7.5 %collective-permute-start.1 = (bf16[96,4,1,160]{0,3,2,1:T(8,128)(2,1)}, bf16[96,4,1,160]{0,3,2,1:T(8,128)(2,1)S(1)}, u32[]{:S(2)}, u32[]{:S(2)}) collective-permute-start(bf16[96,4,1,160]{0,3,2,1:T(8,128)(2,1)} %get-tuple-element.12), channel_id=1, source_target_pairs={{0,4},{1,5},{2,6},{3,7},{8,12},{9,13},{10,14},{11,15},{16,20},{17,... | collective-permute-start | bytes 368648 | tf_op jit(solution)/shard_map/ppermute | solution.py:21
  30.4 0.7 copy-start.2
  31.4 17.7 %copy-start.3 = (bf16[96,4,1,160]{0,3,2,1:T(8,128)(2,1)S(1)}, bf16[96,4,1,160]{0,3,2,1:T(8,128)(2,1)}, u32[]{:S(2)}) copy-start(bf16[96,4,1,160]{0,3,2,1:T(8,128)(2,1)} %copy-done.2) | copy-start | bytes 368644
  31.4 20.0 %copy-start = (bf16[96,2,4,160]{0,3,2,1:T(8,128)(2,1)S(1)}, bf16[96,2,4,160]{0,3,2,1:T(8,128)(2,1)}, u32[]{:S(2)}) copy-start(bf16[96,2,4,160]{0,3,2,1:T(8,128)(2,1)} %param.6) | copy-start | bytes 737284
  76.4 20.5 %copy-start.4 = (bf16[2592,384]{1,0:T(8,128)(2,1)S(1)}, bf16[2592,384]{1,0:T(8,128)(2,1)}, u32[]{:S(2)}) copy-start(bf16[2592,384]{1,0:T(8,128)(2,1)} %reshape.69) | copy-start | bytes 5971972
  97.0 11.1 %copy-start.1 = (bf16[96,2,4,160]{0,3,2,1:T(8,128)(2,1)S(1)}, bf16[96,2,4,160]{0,3,2,1:T(8,128)(2,1)}, u32[]{:S(2)}) copy-start(bf16[96,2,4,160]{0,3,2,1:T(8,128)(2,1)} %param.5) | copy-start | bytes 737284
  105.0 58.7 %copy-start.6 = (f32[384]{0:T(512)S(1)}, f32[384]{0:T(512)}, u32[]{:S(2)}) copy-start(f32[384]{0:T(512)} %param.8) | copy-start | bytes 4612
  105.0 58.7 %copy-start.7 = (f32[384]{0:T(512)S(1)}, f32[384]{0:T(512)}, u32[]{:S(2)}) copy-start(f32[384]{0:T(512)} %param.9) | copy-start | bytes 4612
  108.0 221.1 %all-gather.3.cloned.1.call-start = ((), (), s32[]{:S(2)}) async-start(), calls=%async_computation.1 | async-start | bytes 35831808 | tf_op jit(solution)/shard_map/all_gather | solution.py:53
Sparse Core Ops, SparseCore 0:
  108.1 62.4 reduce-scatter.3
Sparse Core Ops, SparseCore 1:
  173.1 156.0 all-gather.2
